TPU v7x, 32 devices: a whole 2x2x4 slice. The times are simulated.
32 devices in a mesh: sta: 2 (over y), evt: 2 (over core), mode: 8 (over z, x).
Axes of the slice: x: 2, y: 2, z: 4, core: 2. Of those that a mesh axis runs over, the one named last changes fastest.
Arguments:
- receivers: bfloat16 [768, 32768], P('sta', ('mode', 'evt')), may hold values from -6 to 6
- excitations: bfloat16 [32768, 512], P(('mode', 'sta'), 'evt'), may hold values from -0.00390625 to 0.00390625
- mode_freqs: float32 [32768], P('mode'), may hold values from 0 to 1
- mode_damping: float32 [32768], P('mode'), may hold values from 0.02 to 0.2
- sample_freqs: float32 [8], replicated, may hold values from 0.2 to 0.8
Outputs:
- spectra: float32 [768, 2, 8, 512], P(('sta', 'mode'), None, None, 'evt')
All inputs are finite; a program needn't handle non-finite values.
Results may differ from a plain program's by a relative error of at most 0.0029.
Values may be sent and summed in bfloat16 or wider, within the bound.
No kernel may reach another device: no remote copies, remote signals or barrier semaphores. Data moves between devices by JAX's collectives and lax.ppermute only.
A program may use at most 128 MiB of HBM per device.

v0:
```python
import jax
import jax.numpy as jnp
from jax import lax
from jax.sharding import PartitionSpec as P


def resonance(mode_freqs, mode_damping, frequency):
    offset = mode_freqs - frequency
    denominator = offset * offset + mode_damping * mode_damping
    return (mode_damping / denominator, -offset / denominator)


def per_device(receivers, excitations, mode_freqs, mode_damping, sample_freqs):
    receiver_block = lax.all_gather(receivers, "evt", axis=1, tiled=True)
    source_block = lax.all_gather(excitations, "sta", axis=0, tiled=True)
    row_count, mode_count = receiver_block.shape
    real_weight, imag_weight = resonance(
        mode_freqs[None, :], mode_damping[None, :], sample_freqs[:, None]
    )
    weights = jnp.stack([real_weight, imag_weight], axis=0)
    widened = receiver_block.astype(jnp.float32)
    weighted = (widened[:, None, None, :] * weights[None]).astype(jnp.bfloat16)
    partial = jnp.dot(
        weighted.reshape(-1, mode_count), source_block, preferred_element_type=jnp.float32
    )
    partial = partial.reshape(row_count, 2, sample_freqs.shape[0], source_block.shape[1])
    return lax.psum_scatter(partial, "mode", scatter_dimension=0, tiled=True)


def solution(mesh):
    placed = (P("sta", ("mode", "evt")), P(("mode", "sta"), "evt"), P("mode"), P("mode"), P())
    return jax.shard_map(
        per_device,
        mesh=mesh,
        in_specs=placed,
        out_specs=P(("sta", "mode"), None, None, "evt"),
        check_vma=False,
    )
```

profile of v0, /device:TPU:0, one launch (start us, length us, event | category | flops | bytes accessed | tf_op | source)
XLA Modules:
  0.0 204.6 jit_solution(1197653298187763293)
XLA Ops:
  6.5 0.0 all-gather.3.cloned.1.call-start
  6.5 0.7 all-gather.3.cloned.1.call-update
  7.3 0.0 all-gather.5.cloned.1.call-start
  7.3 0.7 all-gather.5.cloned.1.call-update
  8.0 0.0 reduce-scatter.2.cloned.1.call-start
  8.1 0.8 mul.35
  8.9 0.9 fusion.6
  9.7 14.1 %all-gather.3.cloned.1.call-done = bf16[384,4096]{1,0:T(8,128)(2,1)} async-done(((bf16[384,2048]{1,0:T(8,128)(2,1)}), bf16[384,4096]{1,0:T(8,128)(2,1)}) %all-gather.3.cloned.1.call-update) | async-done | bytes 3145744 | tf_op jit(solution)/shard_map/all_gather | solution.py:14
  23.8 5.3 %convert_element_type.8 = f32[384,4096]{1,0:T(8,128)} convert(bf16[384,4096]{1,0:T(8,128)(2,1)} %all-gather.3.cloned.1.call-done) | non-fusion elementwise | flops 1572864 | bytes 9437184 | tf_op jit(solution)/shard_map/convert_element_type | solution.py:21
  29.1 30.5 %all-gather.5.cloned.1.call-done = bf16[4096,256]{1,0:T(8,128)(2,1)} async-done(((bf16[2048,256]{1,0:T(8,128)(2,1)}), bf16[4096,256]{1,0:T(8,128)(2,1)}) %all-gather.5.cloned.1.call-update) | async-done | bytes 2097168 | tf_op jit(solution)/shard_map/all_gather | solution.py:15
  59.7 17.8 %fusion = f32[384,2,8,256]{3,0,2,1:T(8,128)} fusion(f32[2,8,4096]{2,1,0:T(8,128)S(1)} %pad_maximum_fusion, f32[384,4096]{1,0:T(8,128)} %convert_element_type.8, bf16[4096,256]{1,0:T(8,128)(2,1)} %all-gather.5.cloned.1.call-done), kind=kOutput, calls=%fused_computation.1 | convolution fusion | flops 12935233536 | bytes 14942208 | tf_op jit(solution)/shard_map/dot_general | solution.py:23
  77.5 0.0 reduce-scatter.2.cloned.1.call-update
  77.5 118.1 %reduce-scatter.2.cloned.1.call-done = f32[48,2,8,256]{3,0,2,1:T(8,128)} async-done(((f32[384,2,8,256]{3,0,2,1:T(8,128)}), f32[48,2,8,256]{3,0,2,1:T(8,128)}) %reduce-scatter.2.cloned.1.call-update) | async-done | bytes 786448 | tf_op jit(solution)/shard_map/reduce_scatter | solution.py:27
  195.6 2.5 %copy.6 = f32[48,2,8,256]{3,2,1,0:T(8,128)} copy(f32[48,2,8,256]{3,0,2,1:T(8,128)} %reduce-scatter.2.cloned.1.call-done) | data formatting | bytes 1572864 | tf_op jit(solution)/shard_map/reduce_scatter | solution.py:27
  (1 shorter events, 0.0 us)
Async XLA Ops:
  6.5 17.3 %all-gather.3.cloned.1.call-start = ((), (), s32[]{:S(2)}) async-start(), calls=%async_computation.1 | async-start | bytes 4718592 | tf_op jit(solution)/shard_map/all_gather | solution.py:14
  7.3 52.4 %all-gather.5.cloned.1.call-start = ((), (), s32[]{:S(2)}) async-start(), calls=%async_computation.2 | async-start | bytes 3145728 | tf_op jit(solution)/shard_map/all_gather | solution.py:15
  8.0 187.6 %reduce-scatter.2.cloned.1.call-start = ((), (), s32[]{:S(2)}) async-start(), calls=%async_computation.3 | async-start | bytes 7077888 | tf_op jit(solution)/shard_map/reduce_scatter | solution.py:27
Sparse Core Ops, SparseCore 0:
  8.9 14.8 all-gather.2
  25.4 34.2 all-gather.4
  77.7 117.9 reduce-scatter.1
where the time goes:
time: 205 us
  waiting for transfers between devices  164 us (80%)
  matrix products  17.8 us (9%)
  between operations  13.1 us (6%)
  other arithmetic  6.99 us (3%)
  local copies, waits for them, and re-layouts  2.47 us (1%)
    reduce_scatter x1, waiting for transfers between devices, per_device(): return lax.psum_scatter(partial, 'mode', scatter_dimension=0, tiled=True)  118 us
    all_gather x1, waiting for transfers between devices, per_device(): source_block = lax.all_gather(excitations, 'sta', axis=0, tiled=True)  30.5 us
    dot_general x1, matrix products, per_device(): jnp.dot(weighted.reshape(-1, mode_count), source_block, preferred_element...  17.8 us
    all_gather x1, waiting for transfers between devices, per_device(): receiver_block = lax.all_gather(receivers, 'evt', axis=1, tiled=True)  14.1 us
    convert_element_type x1, other arithmetic, per_device(): widened = receiver_block.astype(jnp.float32)  5.32 us
  transfers between devices with their start and end apart: 3, of which 3 were waited for; matrix products, arithmetic and copies ran while one was open for 3% of the time, Pallas kernels for 0%

commit v1 on v0

--- a/solution.py
+++ b/solution.py
@@ -2,6 +2,24 @@
 import jax.numpy as jnp
 from jax import lax
 from jax.sharding import PartitionSpec as P
+
+
+def in_order(blocks, dim):
+    dims = list(blocks.shape[1:])
+    dims[dim] *= blocks.shape[0]
+    return jnp.moveaxis(blocks, 0, dim).reshape(dims)
+
+
+def collected_by_bits(x, axis):
+    count = lax.axis_size(axis)
+    pieces = x[None]
+    for level in range(count.bit_length() - 1):
+        bit = 1 << level
+        partner_block = lax.ppermute(pieces, axis, [(i, i ^ bit) for i in range(count)])
+        both = jnp.stack([pieces, partner_block])
+        upper = lax.axis_index(axis) >> level & 1
+        pieces = jnp.where(upper == 0, both, both[::-1]).reshape(-1, *x.shape)
+    return pieces
 
 
 def resonance(mode_freqs, mode_damping, frequency):
@@ -12,7 +30,7 @@
 
 def per_device(receivers, excitations, mode_freqs, mode_damping, sample_freqs):
     receiver_block = lax.all_gather(receivers, "evt", axis=1, tiled=True)
-    source_block = lax.all_gather(excitations, "sta", axis=0, tiled=True)
+    source_block = in_order(collected_by_bits(excitations, "sta"), 0)
     row_count, mode_count = receiver_block.shape
     real_weight, imag_weight = resonance(
         mode_freqs[None, :], mode_damping[None, :], sample_freqs[:, None]

time: 205 us -> 183 us (0.89)
  waiting for transfers between devices: 164 us -> 142 us
  starting transfers between devices: 0.08 us -> 3.07 us
    all_gather x1 -> x0, waiting for transfers between devices: 30.5 us -> none  [per_device(): source_block = lax.all_gather(excitations, 'sta', axis=0, tiled=True)]
    ppermute x0 -> x1, waiting for transfers between devices: none -> 21.7 us  [collected_by_bits(): lax.ppermute(pieces, axis, [(i, i ^ bit) for i in range(count)])]
    all_gather x1, waiting for transfers between devices: 14.1 us -> 0.02 us  [per_device(): receiver_block = lax.all_gather(receivers, 'evt', axis=1, tiled=True)]
    ppermute x0 -> x1, starting transfers between devices: none -> 3.03 us  [collected_by_bits(): lax.ppermute(pieces, axis, [(i, i ^ bit) for i in range(count)])]
    convert_element_type x1, other arithmetic: 5.32 us -> 2.67 us  [per_device(): widened = receiver_block.astype(jnp.float32)]
  transfers between devices with their start and end apart: 3 -> 3, of which waited for: 3 -> 2; matrix products, arithmetic and copies ran while one was open for 3% -> 1% of each run, Pallas kernels for 0% -> 0%
where the time goes in v1:
time: 183 us; the launch traced here: 182 us
  waiting for transfers between devices  142 us (78%)
  matrix products  16.3 us (9%)
  between operations  13.4 us (7%)
  other arithmetic  5.02 us (3%)
  starting transfers between devices  3.07 us (2%)
  local copies, waits for them, and re-layouts  2.47 us (1%)
    reduce_scatter x1, waiting for transfers between devices, per_device(): return lax.psum_scatter(partial, 'mode', scatter_dimension=0, tiled=True)  120 us
    ppermute x1, waiting for transfers between devices, collected_by_bits(): lax.ppermute(pieces, axis, [(i, i ^ bit) for i in range(count)])  21.7 us
    dot_general x1, matrix products, per_device(): jnp.dot(weighted.reshape(-1, mode_count), source_block, preferred_element...  16.3 us
  transfers between devices with their start and end apart: 3, of which 2 were waited for; matrix products, arithmetic and copies ran while one was open for 1% of the time, Pallas kernels for 0%

profile of v1, /device:TPU:0, one launch (start us, length us, event | category | flops | bytes accessed | tf_op | source)
XLA Modules:
  0.0 182.4 jit_solution(2598148189016808689)
XLA Ops:
  6.5 0.0 copy-start
  6.5 0.0 all-gather.2.cloned.1.call-start
  6.5 0.7 all-gather.2.cloned.1.call-update
  7.3 0.0 reduce-scatter.2.cloned.1.call-start
  7.3 3.0 %collective-permute-start = (bf16[1,2048,256]{2,1,0:T(8,128)(2,1)}, bf16[1,2048,256]{2,1,0:T(8,128)(2,1)S(1)}, u32[]{:S(2)}, u32[]{:S(2)}) collective-permute-start(bf16[1,2048,256]{2,1,0:T(8,128)(2,1)} %bitcast.10), channel_id=1, source_target_pairs={{0,16},{16,0},{1,17},{17,1},{2,18},{18,2},{3,19},{19,3},{4,20},{20... | collective-permute-start | bytes 3145736 | tf_op jit(solution)/shard_map/ppermute | solution.py:18
  10.3 0.8 mul.35
  11.1 0.9 fusion.5
  12.0 21.7 %collective-permute-done = bf16[1,2048,256]{2,1,0:T(8,128)(2,1)S(1)} collective-permute-done((bf16[1,2048,256]{2,1,0:T(8,128)(2,1)}, bf16[1,2048,256]{2,1,0:T(8,128)(2,1)S(1)}, u32[]{:S(2)}, u32[]{:S(2)}) %collective-permute-start) | collective-permute-done | bytes 1048608 | tf_op jit(solution)/shard_map/ppermute | solution.py:18
  33.7 0.0 copy-done
  33.7 0.2 pad_maximum_fusion
  33.9 0.5 reverse_select_fusion
  34.4 0.0 all-gather.2.cloned.1.call-done
  34.4 2.7 %convert_element_type.8 = f32[384,4096]{1,0:T(8,128)S(1)} convert(bf16[384,4096]{1,0:T(8,128)(2,1)} %all-gather.2.cloned.1.call-done) | non-fusion elementwise | flops 1572864 | bytes 9437184 | tf_op jit(solution)/shard_map/convert_element_type | solution.py:39
  37.1 16.3 %fusion = f32[384,2,8,256]{3,0,2,1:T(8,128)} fusion(bf16[4096,256,1,1]{1,0,3,2:T(8,128)(2,1)S(1)} %bitcast.9, f32[2,8,4096]{2,1,0:T(8,128)S(1)} %pad_maximum_fusion.1, f32[384,4096]{1,0:T(8,128)S(1)} %convert_element_type.8), kind=kOutput, calls=%fused_computation.1 | convolution fusion | flops 12935233536 | bytes 14942208 | tf_op jit(solution)/shard_map/dot_general | solution.py:41
  53.4 0.0 reduce-scatter.2.cloned.1.call-update
  53.4 119.6 %reduce-scatter.2.cloned.1.call-done = f32[48,2,8,256]{3,0,2,1:T(8,128)} async-done(((f32[384,2,8,256]{3,0,2,1:T(8,128)}), f32[48,2,8,256]{3,0,2,1:T(8,128)}) %reduce-scatter.2.cloned.1.call-update) | async-done | bytes 786448 | tf_op jit(solution)/shard_map/reduce_scatter | solution.py:45
  173.0 2.5 %copy.6 = f32[48,2,8,256]{3,2,1,0:T(8,128)} copy(f32[48,2,8,256]{3,0,2,1:T(8,128)} %reduce-scatter.2.cloned.1.call-done) | data formatting | bytes 1572864 | tf_op jit(solution)/shard_map/reduce_scatter | solution.py:45
  (1 shorter events, 0.0 us)
Async XLA Ops:
  6.5 27.2 %copy-start = (bf16[2048,256]{1,0:T(8,128)(2,1)S(1)}, bf16[2048,256]{1,0:T(8,128)(2,1)}, u32[]{:S(2)}) copy-start(bf16[2048,256]{1,0:T(8,128)(2,1)} %param.6) | copy-start | bytes 3145732
  6.5 27.9 %all-gather.2.cloned.1.call-start = ((), (), s32[]{:S(2)}) async-start(), calls=%async_computation.1 | async-start | bytes 4718592 | tf_op jit(solution)/shard_map/all_gather | solution.py:32
  7.3 165.8 %reduce-scatter.2.cloned.1.call-start = ((), (), s32[]{:S(2)}) async-start(), calls=%async_computation.2 | async-start | bytes 7077888 | tf_op jit(solution)/shard_map/reduce_scatter | solution.py:45
  7.3 26.4 %collective-permute-start = (bf16[1,2048,256]{2,1,0:T(8,128)(2,1)}, bf16[1,2048,256]{2,1,0:T(8,128)(2,1)S(1)}, u32[]{:S(2)}, u32[]{:S(2)}) collective-permute-start(bf16[1,2048,256]{2,1,0:T(8,128)(2,1)} %bitcast.10), channel_id=1, source_target_pairs={{0,16},{16,0},{1,17},{17,1},{2,18},{18,2},{3,19},{19,3},{4,20},{20... | collective-permute-start | bytes 3145736 | tf_op jit(solution)/shard_map/ppermute | solution.py:18
Sparse Core Ops, SparseCore 0:
  8.9 14.8 all-gather.1
  53.6 119.4 reduce-scatter.1
